TPU v7x, 32 devices: a whole 2x2x4 slice. The times are simulated.
32 devices in a mesh: seq: 4 (over z), ch: 8 (over y, x, core).
Axes of the slice: x: 2, y: 2, z: 4, core: 2. Of those that a mesh axis runs over, the one named last changes fastest.
Arguments:
- inputs: bfloat16 [1024, 8192], P('seq', 'ch'), may hold values from -6 to 6
- w_in: bfloat16 [3, 8192, 8192], P(None, 'seq', 'ch'), may hold values from -0.0625 to 0.0625
- short_filter: float32 [3, 3, 8192], P(None, None, 'ch'), may hold values from -3 to 3
- rates: float32 [16, 8192], P(None, 'ch'), may hold values from 9.765625e-05 to 0.05
- residues: float32 [16, 8192], P(None, 'ch'), may hold values from -3 to 3
- skip: float32 [8192], P('ch'), may hold values from -3 to 3
Outputs:
- gated: bfloat16 [1024, 8192], P('seq', 'ch')
All inputs are finite; a program needn't handle non-finite values.
Results may differ from a plain program's by a relative error of at most 0.0065.
Values may be sent and summed in bfloat16 or wider, within the bound.
No kernel may reach another device: no remote copies, remote signals or barrier semaphores. Data moves between devices by JAX's collectives and lax.ppermute only.
A program may use at most 128 MiB of HBM per device.

v0:
```python
import jax
import jax.numpy as jnp
from jax import lax
from jax.sharding import PartitionSpec as P

TAPS = 3


def passed_along(block, axis, distance):
    devices = range(lax.axis_size(axis))
    route = [(i - distance, i) for i in devices if i - distance in devices]
    return lax.ppermute(block, axis, route)


def carried_in(part, axis, combine, identity):
    place = lax.axis_index(axis)
    gathered = jax.tree.map(lambda a: lax.all_gather(a, axis), part)
    state = jax.tree.map(lambda a, e: jnp.zeros_like(a) + jnp.asarray(e, a.dtype), part, identity)

    def one(hop, state):
        return combine(
            state, jax.tree.map(lambda a: lax.dynamic_index_in_dim(a, hop, 0, False), gathered)
        )

    return lax.fori_loop(0, place, one, state)


def combine(earlier, later):
    return (earlier[0] * later[0], earlier[1] * later[0] + later[1])


def project(inputs, w_in):
    tok_rows = inputs.shape[0]
    n_seq = lax.axis_size("seq")
    n_ch = lax.axis_size("ch")
    features = lax.all_gather(inputs, "ch", axis=1, tiled=True)
    piece = features.shape[1] // (n_seq * n_ch)
    features = features.reshape(tok_rows, n_seq, n_ch, piece)
    mine = lax.dynamic_index_in_dim(features, lax.axis_index("ch"), 2, False)
    rows = lax.all_to_all(mine, "seq", 1, 0, tiled=True)
    rows = rows.reshape(n_seq * tok_rows, piece)
    block = lax.all_gather(rows, "ch", axis=1, tiled=True)
    partial = jnp.einsum("td,kdc->ktc", block, w_in, preferred_element_type=jnp.float32)
    return lax.psum_scatter(partial, "seq", scatter_dimension=1, tiled=True)


def per_device(inputs, w_in, short_filter, rates, residues, skip):
    tok_rows = inputs.shape[0]
    width = w_in.shape[2]
    modes = rates.shape[0]
    proj = project(inputs, w_in).astype(jnp.bfloat16)
    prior = passed_along(proj[:, tok_rows - (TAPS - 1) :, :], "seq", 1)
    padded = jnp.concatenate([prior, proj], axis=1).astype(jnp.float32)
    mixed = jnp.zeros((3, tok_rows, width), jnp.float32)
    for j in range(TAPS):
        mixed = (
            mixed
            + short_filter[:, j, None, :] * padded[:, TAPS - 1 - j : TAPS - 1 - j + tok_rows, :]
        )
    query, key, value = (mixed[0], mixed[1], mixed[2])
    drive = key * value
    position = jnp.arange(tok_rows, dtype=jnp.float32)
    scaled = residues * jnp.sqrt(1.0 - jnp.exp(-2.0 * rates))
    end_powers = jnp.exp(-rates[None, :, :] * (tok_rows - 1.0 - position)[:, None, None])
    end_state = jnp.sum(end_powers * drive[:, None, :], axis=0)
    block_decay = jnp.exp(-rates * tok_rows)
    identity = (jnp.ones_like(block_decay), jnp.zeros_like(end_state))
    entering = carried_in((block_decay, end_state), "seq", combine, identity)[1]
    start_powers = jnp.exp(-rates[None, :, :] * (position + 1.0)[:, None, None])
    cross = jnp.sum(start_powers * (scaled * entering)[None, :, :], axis=1)
    center = (tok_rows - 1.0) / 2.0
    offset = (position - center)[:, None, None]
    rising = jnp.exp(rates[None, :, :] * offset) * drive[:, None, :]
    offsets = jnp.arange(tok_rows, dtype=jnp.int32)
    lower = (offsets[:, None] >= offsets[None, :]).astype(jnp.float32)
    prefix = jnp.dot(
        lower, rising.reshape(tok_rows, modes * width), precision=lax.Precision.HIGHEST
    )
    prefix = prefix.reshape(tok_rows, modes, width)
    falling = jnp.exp(-rates[None, :, :] * offset) * scaled[None, :, :]
    local = jnp.sum(falling * prefix, axis=1)
    return (query * (local + cross + skip[None, :] * drive)).astype(jnp.bfloat16)


def solution(mesh):
    in_specs = (
        P("seq", "ch"),
        P(None, "seq", "ch"),
        P(None, None, "ch"),
        P(None, "ch"),
        P(None, "ch"),
        P("ch"),
    )
    out_specs = P("seq", "ch")
    return jax.shard_map(
        per_device, mesh=mesh, in_specs=in_specs, out_specs=out_specs, check_vma=False
    )
```

profile of v0, /device:TPU:26, one launch (start us, length us, event | category | flops | bytes accessed | tf_op | source)
XLA Modules:
  0.0 415.0 jit_solution(5616361309072354084)
XLA Ops:
  6.5 0.7 all-gather.5.cloned.1.call-update
  7.3 0.0 all-gather.7.cloned.1.call-start
  7.3 39.5 %all-gather.5.cloned.1.call-done = bf16[256,8192]{1,0:T(8,128)(2,1)} async-done(((bf16[256,1024]{1,0:T(8,128)(2,1)}), bf16[256,8192]{1,0:T(8,128)(2,1)}) %all-gather.5.cloned.1.call-update) | async-done | bytes 4194320 | tf_op jit(solution)/shard_map/all_gather | solution.py:36
  46.8 3.6 copy.15
  50.4 1.1 constant_dynamic-slice_fusion
  51.5 0.2 copy.21
  51.7 17.5 %all_to_all.15 = bf16[256,4,256]{2,0,1:T(8,128)(2,1)} all-to-all(bf16[256,4,256]{2,0,1:T(8,128)(2,1)S(1)} %bitcast.60), channel_id=1, replica_groups=mesh['seq'=4,'ch'=8] {'seq'}, dimensions={1} | all-to-all | bytes 1048576 | tf_op jit(solution)/shard_map/all_to_all | solution.py:40
  69.2 0.0 reduce-scatter.2.cloned.1.call-start
  69.3 37.4 %all-gather.7.cloned.1.call-done = bf16[1024,2048]{1,0:T(8,128)(2,1)} async-done(((bf16[1024,256]{1,0:T(8,128)(2,1)}), bf16[1024,2048]{1,0:T(8,128)(2,1)}) %all-gather.7.cloned.1.call-update) | async-done | bytes 4194320 | tf_op jit(solution)/shard_map/all_gather | solution.py:42
  106.7 18.9 %convolution_bitcast_fusion = f32[3,1024,1024]{2,1,0:T(8,128)} fusion(bf16[3,2048,1024]{2,1,0:T(8,128)(2,1)} %param.9, bf16[1024,2048]{1,0:T(8,128)(2,1)} %all-gather.7.cloned.1.call-done), kind=kOutput, calls=%fused_computation.6 | convolution fusion | flops 12884901888 | bytes 29360128 | tf_op jit(solution)/shard_map/td,kdc->ktc/dot_general | solution.py:43
  125.7 0.7 copy-done.2
  126.5 0.6 fusion.9
  127.1 210.6 %reduce-scatter.2.cloned.1.call-done = f32[3,256,1024]{2,1,0:T(8,128)} async-done(((f32[3,1024,1024]{2,1,0:T(8,128)}), f32[3,256,1024]{2,1,0:T(8,128)}) %reduce-scatter.2.cloned.1.call-update) | async-done | bytes 3145744 | tf_op jit(solution)/shard_map/reduce_scatter | solution.py:44
  337.7 2.1 convert_element_type.10
  339.9 1.3 collective-permute-start
  341.2 15.8 %all-gather = f32[64,1024]{1,0:T(8,128)S(1)} all-gather(f32[16,1024]{1,0:T(8,128)S(1)} %get-tuple-element.63), channel_id=2, replica_groups=mesh['seq'=4,'ch'=8] {'seq'}, dimensions={0}, use_global_device_ids=true | all-gather | bytes 327680 | tf_op jit(solution)/shard_map/all_gather | solution.py:17
  357.0 0.6 copy.16
  357.6 0.5 maximum_convert_fusion
  358.1 0.9 fusion.1
  359.0 1.2 fusion.3
  360.2 2.5 copy.14
  362.7 4.1 multiply_reduce_fusion.1
  366.8 14.6 %all-gather.1 = f32[64,1024]{1,0:T(8,128)} all-gather(f32[16,1024]{1,0:T(8,128)S(1)} %multiply_reduce_fusion.1), channel_id=3, replica_groups=mesh['seq'=4,'ch'=8] {'seq'}, dimensions={0}, use_global_device_ids=true | all-gather | bytes 327680 | tf_op jit(solution)/shard_map/all_gather | solution.py:17
  381.4 2.9 while.12
  381.4 0.9 bitcast_add_fusion.2
  382.3 0.9 bitcast_add_fusion.2
  383.2 0.9 bitcast_add_fusion.2
  384.3 0.9 fusion.8
  385.2 3.9 bitcast_multiply_fusion.1
  389.2 13.9 %multiply_reduce_fusion.2 = f32[256,1024]{1,0:T(8,128)} fusion(f32[16,1024,256]{2,1,0:T(8,128)S(1)} %bitcast.57, f32[16,1024]{1,0:T(8,128)S(1)} %get-tuple-element.61, f32[256]{0:T(256)S(1)} %iota_add_fusion.1, f32[16,1024]{1,0:T(8,128)S(1)} %copy-done.1), kind=kOutput, calls=%fused_computation.5 | convolution fusion | flops 12901482496 | bytes 17957888 | tf_op jit(solution)/shard_map/dot_general | solution.py:76
  403.1 2.8 multiply_reduce_fusion
  405.9 2.6 fusion.5
  (19 shorter events, 0.2 us)
Async XLA Ops:
  6.5 40.3 %all-gather.5.cloned.1.call-start = ((), (), s32[]{:S(2)}) async-start(), calls=%async_computation.2 | async-start | bytes 4718592 | tf_op jit(solution)/shard_map/all_gather | solution.py:36
  7.3 99.5 %all-gather.7.cloned.1.call-start = ((), (), s32[]{:S(2)}) async-start(), calls=%async_computation.3 | async-start | bytes 4718592 | tf_op jit(solution)/shard_map/all_gather | solution.py:42
  69.2 268.5 %reduce-scatter.2.cloned.1.call-start = ((), (), s32[]{:S(2)}) async-start(), calls=%async_computation.4 | async-start | bytes 15728640 | tf_op jit(solution)/shard_map/reduce_scatter | solution.py:44
  125.6 0.8 copy-start.2
  125.6 0.9 copy-start
  339.9 17.7 %collective-permute-start = (bf16[3,2,1024]{2,1,0:T(2,128)(2,1)S(1)}, bf16[3,2,1024]{2,1,0:T(2,128)(2,1)S(1)}, u32[]{:S(2)}, u32[]{:S(2)}) collective-permute-start(bf16[3,2,1024]{2,1,0:T(2,128)(2,1)S(1)} %slice.40), channel_id=1, source_target_pairs={{0,8},{8,16},{16,24},{1,9},{9,17},{17,25},{2,10},{10,18},{18,26},{... | collective-permute-start | bytes 36872 | tf_op jit(solution)/shard_map/ppermute | solution.py:12
  384.3 4.8 %copy-start.1 = (f32[16,1024]{1,0:T(8,128)S(1)}, f32[16,1024]{1,0:T(8,128)}, u32[]{:S(2)}) copy-start(f32[16,1024]{1,0:T(8,128)} %get-tuple-element.62) | copy-start | bytes 196612
  389.1 16.7 %copy-start.3 = (f32[1024]{0:T(1024)S(1)}, f32[1024]{0:T(1024)}, u32[]{:S(2)}) copy-start(f32[1024]{0:T(1024)} %param.13) | copy-start | bytes 12292
Sparse Core Ops, SparseCore 0:
  9.2 37.5 all-gather.4
  69.3 37.3 all-gather.6
  125.8 211.8 reduce-scatter.1
where the time goes:
time: 416 us; the launch traced here: 415 us
  waiting for transfers between devices  288 us (69%)
  blocking collectives  47.9 us (12%)
  matrix products  32.8 us (8%)
  other arithmetic  22.3 us (5%)
  between operations  13.3 us (3%)
  local copies, waits for them, and re-layouts  8.82 us (2%)
    reduce_scatter x1, waiting for transfers between devices, project(): return lax.psum_scatter(partial, 'seq', scatter_dimension=1, tiled=True)  211 us
    all_gather x1, waiting for transfers between devices, project(): features = lax.all_gather(inputs, 'ch', axis=1, tiled=True)  39.5 us
    all_gather x1, waiting for transfers between devices, project(): block = lax.all_gather(rows, 'ch', axis=1, tiled=True)  37.4 us
    all_gather x2, blocking collectives, carried_in(): gathered = jax.tree.map(lambda a: lax.all_gather(a, axis), part)  30.4 us
    dot_general x1, matrix products, project(): jnp.einsum('td,kdc->ktc', block, w_in, preferred_element_type=jnp.float32)  18.9 us
    all_to_all x1, blocking collectives, project(): rows = lax.all_to_all(mine, 'seq', 1, 0, tiled=True)  17.5 us
    dot_general x1, matrix products, per_device(): jnp.dot(lower, rising.reshape(tok_rows, modes * width), precision=lax.Pre...  13.9 us
  transfers between devices with their start and end apart: 4, of which 3 were waited for; matrix products, arithmetic and copies ran while one was open for 0% of the time, Pallas kernels for 0%

commit v1 on v0

--- a/solution.py
+++ b/solution.py
@@ -4,6 +4,27 @@
 from jax.sharding import PartitionSpec as P
 
 TAPS = 3
+
+
+def ring_gather(array, axis, dim):
+    size, position, rows = (lax.axis_size(axis), lax.axis_index(axis), array.shape[dim])
+    ahead = [(i, (i + 1) % size) for i in range(size)]
+    downward = [(i, (i - 1) % size) for i in range(size)]
+    out = jnp.zeros((*array.shape[:dim], size * rows, *array.shape[dim + 1 :]), array.dtype)
+    out = lax.dynamic_update_slice_in_dim(out, array, position * rows, axis=dim)
+    from_left = from_right = array
+    halfway = size // 2
+    for turn in range(1, halfway + 1):
+        from_left = lax.ppermute(from_left, axis, ahead)
+        out = lax.dynamic_update_slice_in_dim(
+            out, from_left, (position - turn) % size * rows, axis=dim
+        )
+        if turn < size - halfway:
+            from_right = lax.ppermute(from_right, axis, downward)
+            out = lax.dynamic_update_slice_in_dim(
+                out, from_right, (position + turn) % size * rows, axis=dim
+            )
+    return out
 
 
 def passed_along(block, axis, distance):
@@ -39,7 +60,7 @@
     mine = lax.dynamic_index_in_dim(features, lax.axis_index("ch"), 2, False)
     rows = lax.all_to_all(mine, "seq", 1, 0, tiled=True)
     rows = rows.reshape(n_seq * tok_rows, piece)
-    block = lax.all_gather(rows, "ch", axis=1, tiled=True)
+    block = ring_gather(rows, "ch", 1)
     partial = jnp.einsum("td,kdc->ktc", block, w_in, preferred_element_type=jnp.float32)
     return lax.psum_scatter(partial, "seq", scatter_dimension=1, tiled=True)
 

time: 416 us -> 424 us (1.019)
  starting transfers between devices: 1.37 us -> 20 us
  waiting for transfers between devices: 288 us -> 282 us
    all_gather x1 -> x0, waiting for transfers between devices: 37.4 us -> none  [project(): block = lax.all_gather(rows, 'ch', axis=1, tiled=True)]
    ppermute x0 -> x7, waiting for transfers between devices: none -> 26.2 us  [the longest x4 25.7 us: ring_gather(): from_left = lax.ppermute(from_left, axis, ahead)]
    ppermute x0 -> x7, starting transfers between devices: none -> 18.7 us  [the longest x4 13.4 us: ring_gather(): from_left = lax.ppermute(from_left, axis, ahead)]
    reduce_scatter x1, waiting for transfers between devices: 211 us -> 218 us  [project(): return lax.psum_scatter(partial, 'seq', scatter_dimension=1, tiled=True)]
  transfers between devices with their start and end apart: 4 -> 10, of which waited for: 3 -> 7; matrix products, arithmetic and copies ran while one was open for 0% -> 1% of each run, Pallas kernels for 0% -> 0%
where the time goes in v1:
time: 424 us; the launch traced here: 423 us
  waiting for transfers between devices  282 us (67%)
  blocking collectives  47.8 us (11%)
  matrix products  29.5 us (7%)
  other arithmetic  21 us (5%)
  starting transfers between devices  20 us (5%)
  between operations  13.7 us (3%)
  local copies, waits for them, and re-layouts  8.38 us (2%)
    reduce_scatter x1, waiting for transfers between devices, project(): return lax.psum_scatter(partial, 'seq', scatter_dimension=1, tiled=True)  218 us
    all_gather x1, waiting for transfers between devices, project(): features = lax.all_gather(inputs, 'ch', axis=1, tiled=True)  38.1 us
    all_gather x2, blocking collectives, carried_in(): gathered = jax.tree.map(lambda a: lax.all_gather(a, axis), part)  30.4 us
    ppermute x4, waiting for transfers between devices, ring_gather(): from_left = lax.ppermute(from_left, axis, ahead)  25.7 us
    all_to_all x1, blocking collectives, project(): rows = lax.all_to_all(mine, 'seq', 1, 0, tiled=True)  17.4 us
    dot_general x1, matrix products, project(): jnp.einsum('td,kdc->ktc', block, w_in, preferred_element_type=jnp.float32)  15.5 us
    dot_general x1, matrix products, per_device(): jnp.dot(lower, rising.reshape(tok_rows, modes * width), precision=lax.Pre...  14 us
    ppermute x4, starting transfers between devices, ring_gather(): from_left = lax.ppermute(from_left, axis, ahead)  13.4 us
  transfers between devices with their start and end apart: 10, of which 7 were waited for; matrix products, arithmetic and copies ran while one was open for 1% of the time, Pallas kernels for 0%

profile of v1, /device:TPU:26, one launch (start us, length us, event | category | flops | bytes accessed | tf_op | source)
XLA Modules:
  0.0 422.7 jit_solution(1415495555207602423)
XLA Ops:
  6.5 2.0 copy.8
  8.7 38.1 %all-gather.4.cloned.1.call-done = bf16[256,8192]{0,1:T(8,128)(2,1)} async-done(((bf16[256,1024]{0,1:T(8,128)(2,1)}), bf16[256,8192]{0,1:T(8,128)(2,1)}) %all-gather.4.cloned.1.call-update) | async-done | bytes 4194320 | tf_op jit(solution)/shard_map/all_gather | solution.py:57
  46.8 1.1 constant_dynamic-slice_fusion
  48.1 17.4 %all_to_all.15 = bf16[256,4,256]{2,0,1:T(8,128)(2,1)S(1)} all-to-all(bf16[256,4,256]{2,0,1:T(8,128)(2,1)S(1)} %bitcast.57), channel_id=1, replica_groups=mesh['seq'=4,'ch'=8] {'seq'}, dimensions={1} | all-to-all | bytes 1048576 | tf_op jit(solution)/shard_map/all_to_all | solution.py:61
  65.5 1.7 collective-permute-start.1
  67.3 10.7 %collective-permute-done = bf16[1024,256]{1,0:T(8,128)(2,1)S(1)} collective-permute-done((bf16[1024,256]{1,0:T(8,128)(2,1)S(1)}, bf16[1024,256]{1,0:T(8,128)(2,1)S(1)}, u32[]{:S(2)}, u32[]{:S(2)}) %collective-permute-start) | collective-permute-done | bytes 524320 | tf_op jit(solution)/shard_map/ppermute | solution.py:18
  78.5 1.9 collective-permute-start.3
  80.5 8.2 %collective-permute-done.2 = bf16[1024,256]{1,0:T(8,128)(2,1)S(1)} collective-permute-done((bf16[1024,256]{1,0:T(8,128)(2,1)S(1)}, bf16[1024,256]{1,0:T(8,128)(2,1)S(1)}, u32[]{:S(2)}, u32[]{:S(2)}) %collective-permute-start.2) | collective-permute-done | bytes 524320 | tf_op jit(solution)/shard_map/ppermute | solution.py:18
  88.6 4.0 collective-permute-start.4
  93.2 1.6 collective-permute-start.5
  94.9 2.9 collective-permute-done.4
  97.8 9.5 %collective-permute-start.6 = (bf16[1024,256]{1,0:T(8,128)(2,1)S(1)}, bf16[1024,256]{1,0:T(8,128)(2,1)S(1)}, u32[]{:S(2)}, u32[]{:S(2)}) collective-permute-start(bf16[1024,256]{1,0:T(8,128)(2,1)S(1)} %collective-permute-done.4), channel_id=1, source_target_pairs={{0,1},{1,2},{2,3},{3,4},{4,5},{5,6},{6,7},{7,0},{8,9},{9,10},{10,1... | collective-permute-start | bytes 1572872 | tf_op jit(solution)/shard_map/ppermute | solution.py:18
  107.7 3.8 collective-permute-done.6
  111.6 15.5 %convolution_bitcast_fusion = f32[3,1024,1024]{2,1,0:T(8,128)} fusion(bf16[3,2048,1024]{2,1,0:T(8,128)(2,1)S(1)} %copy-done.6, bf16[1024,2048]{1,0:T(8,128)(2,1)S(1)} %constant_dynamic-update-slice_fusion), kind=kOutput, calls=%fused_computation.6 | convolution fusion | flops 12884901888 | bytes 29360128 | tf_op jit(solution)/shard_map/td,kdc->ktc/dot_general | solution.py:64
  128.6 217.7 %reduce-scatter.2.cloned.1.call-done = f32[3,256,1024]{2,1,0:T(8,128)} async-done(((f32[3,1024,1024]{2,1,0:T(8,128)}), f32[3,256,1024]{2,1,0:T(8,128)}) %reduce-scatter.2.cloned.1.call-update) | async-done | bytes 3145744 | tf_op jit(solution)/shard_map/reduce_scatter | solution.py:65
  346.2 2.1 convert_element_type.10
  348.4 1.3 collective-permute-start.7
  349.7 15.8 %all-gather = f32[64,1024]{1,0:T(8,128)S(1)} all-gather(f32[16,1024]{1,0:T(8,128)S(1)} %get-tuple-element.63), channel_id=2, replica_groups=mesh['seq'=4,'ch'=8] {'seq'}, dimensions={0}, use_global_device_ids=true | all-gather | bytes 327680 | tf_op jit(solution)/shard_map/all_gather | solution.py:38
  366.6 0.9 fusion.1
  367.5 1.1 fusion.3
  368.7 2.5 copy.15
  371.2 4.1 multiply_reduce_fusion.1
  375.3 14.6 %all-gather.1 = f32[64,1024]{1,0:T(8,128)} all-gather(f32[16,1024]{1,0:T(8,128)S(1)} %multiply_reduce_fusion.1), channel_id=3, replica_groups=mesh['seq'=4,'ch'=8] {'seq'}, dimensions={0}, use_global_device_ids=true | all-gather | bytes 327680 | tf_op jit(solution)/shard_map/all_gather | solution.py:38
  390.0 2.9 while.12
  390.0 0.9 bitcast_add_fusion.2
  390.9 0.9 bitcast_add_fusion.2
  391.8 0.9 bitcast_add_fusion.2
  392.8 0.9 fusion.8
  393.7 3.9 bitcast_multiply_fusion.1
  397.7 14.0 %multiply_reduce_fusion.2 = f32[256,1024]{1,0:T(8,128)} fusion(f32[16,1024,256]{2,1,0:T(8,128)S(1)} %bitcast.53, f32[16,1024]{1,0:T(8,128)S(1)} %get-tuple-element.61, f32[256]{0:T(256)S(1)} %iota_add_fusion.1, f32[16,1024]{1,0:T(8,128)S(1)} %copy-done.3), kind=kOutput, calls=%fused_computation.5 | convolution fusion | flops 12901482496 | bytes 17957888 | tf_op jit(solution)/shard_map/dot_general | solution.py:97
  411.7 2.8 multiply_reduce_fusion
  414.5 1.4 fusion.5
  (45 shorter events, 4.5 us)
Async XLA Ops:
  6.5 40.3 %all-gather.4.cloned.1.call-start = ((), (), s32[]{:S(2)}) async-start(), calls=%async_computation.2 | async-start | bytes 4718592 | tf_op jit(solution)/shard_map/all_gather | solution.py:57
  8.6 337.6 %reduce-scatter.2.cloned.1.call-start = ((), (), s32[]{:S(2)}) async-start(), calls=%async_computation.3 | async-start | bytes 15728640 | tf_op jit(solution)/shard_map/reduce_scatter | solution.py:65
  65.5 12.5 %collective-permute-start = (bf16[1024,256]{1,0:T(8,128)(2,1)S(1)}, bf16[1024,256]{1,0:T(8,128)(2,1)S(1)}, u32[]{:S(2)}, u32[]{:S(2)}) collective-permute-start(bf16[1024,256]{1,0:T(8,128)(2,1)S(1)} %bitcast.54), channel_id=1, source_target_pairs={{0,1},{1,2},{2,3},{3,4},{4,5},{5,6},{6,7},{7,0},{8,9},{9,10},{10,1... | collective-permute-start | bytes 1572872 | tf_op jit(solution)/shard_map/ppermute | solution.py:18
  65.5 13.0 %collective-permute-start.1 = (bf16[1024,256]{1,0:T(8,128)(2,1)S(1)}, bf16[1024,256]{1,0:T(8,128)(2,1)S(1)}, u32[]{:S(2)}, u32[]{:S(2)}) collective-permute-start(bf16[1024,256]{1,0:T(8,128)(2,1)S(1)} %bitcast.55), channel_id=1, source_target_pairs={{0,7},{1,0},{2,1},{3,2},{4,3},{5,4},{6,5},{7,6},{8,15},{9,8},{10,9... | collective-permute-start | bytes 1572872 | tf_op jit(solution)/shard_map/ppermute | solution.py:23
  78.0 10.7 %collective-permute-start.2 = (bf16[1024,256]{1,0:T(8,128)(2,1)S(1)}, bf16[1024,256]{1,0:T(8,128)(2,1)S(1)}, u32[]{:S(2)}, u32[]{:S(2)}) collective-permute-start(bf16[1024,256]{1,0:T(8,128)(2,1)S(1)} %collective-permute-done), channel_id=1, source_target_pairs={{0,1},{1,2},{2,3},{3,4},{4,5},{5,6},{6,7},{7,0},{8,9},{9,10},{10,1... | collective-permute-start | bytes 1572872 | tf_op jit(solution)/shard_map/ppermute | solution.py:18
  78.5 14.7 %collective-permute-start.3 = (bf16[1024,256]{1,0:T(8,128)(2,1)S(1)}, bf16[1024,256]{1,0:T(8,128)(2,1)S(1)}, u32[]{:S(2)}, u32[]{:S(2)}) collective-permute-start(bf16[1024,256]{1,0:T(8,128)(2,1)S(1)} %collective-permute-done.1), channel_id=1, source_target_pairs={{0,7},{1,0},{2,1},{3,2},{4,3},{5,4},{6,5},{7,6},{8,15},{9,8},{10,9... | collective-permute-start | bytes 1572872 | tf_op jit(solution)/shard_map/ppermute | solution.py:23
  88.6 9.2 %collective-permute-start.4 = (bf16[1024,256]{1,0:T(8,128)(2,1)S(1)}, bf16[1024,256]{1,0:T(8,128)(2,1)S(1)}, u32[]{:S(2)}, u32[]{:S(2)}) collective-permute-start(bf16[1024,256]{1,0:T(8,128)(2,1)S(1)} %collective-permute-done.2), channel_id=1, source_target_pairs={{0,1},{1,2},{2,3},{3,4},{4,5},{5,6},{6,7},{7,0},{8,9},{9,10},{10,1... | collective-permute-start | bytes 1572872 | tf_op jit(solution)/shard_map/ppermute | solution.py:18
  92.6 18.9 %copy-start.6 = (bf16[3,2048,1024]{2,1,0:T(8,128)(2,1)S(1)}, bf16[3,2048,1024]{2,1,0:T(8,128)(2,1)}, u32[]{:S(2)}) copy-start(bf16[3,2048,1024]{2,1,0:T(8,128)(2,1)} %param.9) | copy-start | bytes 37748740
  93.2 14.3 %collective-permute-start.5 = (bf16[1024,256]{1,0:T(8,128)(2,1)S(1)}, bf16[1024,256]{1,0:T(8,128)(2,1)S(1)}, u32[]{:S(2)}, u32[]{:S(2)}) collective-permute-start(bf16[1024,256]{1,0:T(8,128)(2,1)S(1)} %collective-permute-done.3), channel_id=1, source_target_pairs={{0,7},{1,0},{2,1},{3,2},{4,3},{5,4},{6,5},{7,6},{8,15},{9,8},{10,9... | collective-permute-start | bytes 1572872 | tf_op jit(solution)/shard_map/ppermute | solution.py:23
  97.8 13.7 %collective-permute-start.6 = (bf16[1024,256]{1,0:T(8,128)(2,1)S(1)}, bf16[1024,256]{1,0:T(8,128)(2,1)S(1)}, u32[]{:S(2)}, u32[]{:S(2)}) collective-permute-start(bf16[1024,256]{1,0:T(8,128)(2,1)S(1)} %collective-permute-done.4), channel_id=1, source_target_pairs={{0,1},{1,2},{2,3},{3,4},{4,5},{5,6},{6,7},{7,0},{8,9},{9,10},{10,1... | collective-permute-start | bytes 1572872 | tf_op jit(solution)/shard_map/ppermute | solution.py:18
  127.1 0.8 copy-start.4
  127.1 0.9 copy-start.1
  348.4 17.7 %collective-permute-start.7 = (bf16[3,2,1024]{2,1,0:T(2,128)(2,1)S(1)}, bf16[3,2,1024]{2,1,0:T(2,128)(2,1)S(1)}, u32[]{:S(2)}, u32[]{:S(2)}) collective-permute-start(bf16[3,2,1024]{2,1,0:T(2,128)(2,1)S(1)} %slice.40), channel_id=1, source_target_pairs={{0,8},{8,16},{16,24},{1,9},{9,17},{17,25},{2,10},{10,18},{18,26},{... | collective-permute-start | bytes 36872 | tf_op jit(solution)/shard_map/ppermute | solution.py:33
  367.5 3.7 copy-start.2
  393.7 3.9 copy-start.3
  411.7 2.8 copy-start
  411.7 2.8 copy-start.5
Sparse Core Ops, SparseCore 0:
  9.2 37.5 all-gather.3
  127.2 218.9 reduce-scatter.1
